TPU v7x, 256 devices: a whole 4x4x8 slice. The times are simulated.
256 devices in a mesh: vel: 16 (over y, z_lo), space: 16 (over x, z_hi, core).
Axes of the slice: x: 4, y: 4, z: 8 (z_hi: 2, z_lo: 4; z = z_hi * 4 + z_lo), core: 2. Of those that a mesh axis runs over, the one named last changes fastest.
Arguments:
- initial: float32 [13824, 64, 128], P('vel', 'space'), as said below
- site_kind: int32 [64, 128], P('space'), may hold values from 0 to 2, as said below
Outputs:
- distribution: float32 [13824, 64, 128], P('vel', 'space')
- kelvin_level: float32 [64, 128], P('space')
Inputs may be any that keep to these rules, and one draw needn't show every extreme that they name: `site_kind`: 0 marks a gas cell, 1 a wall cell, 2 an inflow cell. `initial`: every entry is positive.
All inputs are finite; a program needn't handle non-finite values.
Results may differ from a plain program's by a relative error of at most 0.0003.
Values sent between devices are 32-bit elements; how exact they have to be, the bound alone decides.
No kernel may reach another device: no remote copies, remote signals or barrier semaphores. Data moves between devices by JAX's collectives and lax.ppermute only.
A program may use at most 64 MiB of HBM per device.

v0:
```python
import math
import jax
import jax.numpy as jnp
from jax import lax
from jax.sharding import PartitionSpec as P

NVX = 24
STEPS = 2
speed_limit = 4.0
courant = 0.1
diffusivity_ratio = 2.0 / 3.0
power_law_index = 0.81
encounter_rate = 0.25
wall_kelvin = 1.0
inflow_concentration = 1.0
inflow_speed = 0.5
inflow_kelvin = 1.0


def with_halo(block, sides, width):
    for axis, dim in sides:
        count = lax.axis_size(axis)
        forward = [(i, i + 1) for i in range(count - 1)]
        backward = [(target, source) for source, target in forward]
        low = lax.ppermute(
            lax.slice_in_dim(block, block.shape[dim] - width, None, axis=dim), axis, forward
        )
        high = lax.ppermute(lax.slice_in_dim(block, 0, width, axis=dim), axis, backward)
        block = jnp.concatenate([low, block, high], axis=dim)
    return block


def speeds(offset, amount):
    index = offset + jnp.arange(amount, dtype=jnp.int32)
    spacing = 2.0 * speed_limit / (NVX - 1)
    along_x_part = -speed_limit + spacing * (index // (NVX * NVX)).astype(jnp.float32)
    along_y_part = -speed_limit + spacing * (index // NVX % NVX).astype(jnp.float32)
    along_z_part = -speed_limit + spacing * (index % NVX).astype(jnp.float32)
    return (along_x_part, along_y_part, along_z_part)


def quad_weight():
    return (2.0 * speed_limit / (NVX - 1)) ** 3 / (2.0 * math.pi) ** 1.5


def minmod(left, right):
    return 0.5 * (jnp.sign(left) + jnp.sign(right)) * jnp.minimum(jnp.abs(left), jnp.abs(right))


def sweep(distribution_table, number, along):
    length = distribution_table.shape[along]

    def piece(source, low, high):
        return lax.slice_in_dim(source, low, high, axis=along)

    jumps = piece(distribution_table, 1, length) - piece(distribution_table, 0, length - 1)
    slopes = minmod(piece(jumps, 0, length - 2), piece(jumps, 1, length - 1))
    left_face = piece(distribution_table, 1, length - 2) + 0.5 * (1.0 - number) * piece(
        slopes, 0, length - 3
    )
    right_face = piece(distribution_table, 2, length - 1) - 0.5 * (1.0 + number) * piece(
        slopes, 1, length - 2
    )
    flux = number * jnp.where(number > 0, left_face, right_face)
    return piece(distribution_table, 2, length - 2) - (
        piece(flux, 1, length - 3) - piece(flux, 0, length - 4)
    )


def transport(padded, along_x_part, along_y_part):
    swept = sweep(padded, courant * along_x_part[:, None, None], 1)
    widened = jnp.pad(swept, ((0, 0), (0, 0), (2, 2)))
    return sweep(widened, courant * along_y_part[:, None, None], 2)


def macroscopic_moments(advected_distribution, along_x_part, along_y_part, along_z_part):
    magnitude_squares = (
        along_x_part * along_x_part + along_y_part * along_y_part + along_z_part * along_z_part
    )
    ones = jnp.ones_like(along_x_part)
    table = quad_weight() * jnp.stack(
        [ones, along_x_part, along_y_part, along_z_part, magnitude_squares]
    )
    local = jnp.einsum("kv,vrc->krc", table, advected_distribution, precision=lax.Precision.HIGHEST)
    integral_totals = lax.psum(local, "vel")
    particle_concentration = integral_totals[0]
    average_drift_x = integral_totals[1] / particle_concentration
    average_drift_y = integral_totals[2] / particle_concentration
    average_drift_z = integral_totals[3] / particle_concentration
    kelvin_level = (
        integral_totals[4] / particle_concentration
        - (
            average_drift_x * average_drift_x
            + average_drift_y * average_drift_y
            + average_drift_z * average_drift_z
        )
    ) / 3.0
    rel_x = along_x_part[:, None, None] - average_drift_x[None]
    rel_y = along_y_part[:, None, None] - average_drift_y[None]
    rel_z = along_z_part[:, None, None] - average_drift_z[None]
    scaled = (
        0.5
        * quad_weight()
        * (rel_x * rel_x + rel_y * rel_y + rel_z * rel_z)
        * advected_distribution
    )
    local_heat = jnp.stack(
        [
            jnp.sum(rel_x * scaled, axis=0),
            jnp.sum(rel_y * scaled, axis=0),
            jnp.sum(rel_z * scaled, axis=0),
        ]
    )
    conductive_transfer = lax.psum(local_heat, "vel")
    return (
        particle_concentration,
        average_drift_x,
        average_drift_y,
        average_drift_z,
        kelvin_level,
        conductive_transfer,
    )


def approach_increment(
    advected_distribution, kind_labels, along_x_part, along_y_part, along_z_part
):
    (
        particle_concentration,
        average_drift_x,
        average_drift_y,
        average_drift_z,
        kelvin_level,
        conductive_transfer,
    ) = macroscopic_moments(advected_distribution, along_x_part, along_y_part, along_z_part)
    rel_x = along_x_part[:, None, None] - average_drift_x[None]
    rel_y = along_y_part[:, None, None] - average_drift_y[None]
    rel_z = along_z_part[:, None, None] - average_drift_z[None]
    relative_magnitude_square = rel_x * rel_x + rel_y * rel_y + rel_z * rel_z
    stress_scalar_grid = particle_concentration * kelvin_level
    gaussian_local_balance = (
        particle_concentration
        * kelvin_level ** (-1.5)
        * jnp.exp(-relative_magnitude_square / (2.0 * kelvin_level))
    )
    conductive_vector_slot = (
        rel_x * conductive_transfer[0]
        + rel_y * conductive_transfer[1]
        + rel_z * conductive_transfer[2]
    )
    corrected_goal_distribution = gaussian_local_balance * (
        1.0
        + (1.0 - diffusivity_ratio)
        * conductive_vector_slot
        * (relative_magnitude_square / kelvin_level - 5.0)
        / (5.0 * stress_scalar_grid * kelvin_level)
    )
    approach_rate = (
        encounter_rate * particle_concentration * kelvin_level ** (1.0 - power_law_index)
    )
    relaxed = advected_distribution + approach_rate * (
        corrected_goal_distribution - advected_distribution
    )
    magnitude_squares = (
        along_x_part * along_x_part + along_y_part * along_y_part + along_z_part * along_z_part
    )[:, None, None]
    wall_distribution = (
        particle_concentration
        * wall_kelvin ** (-1.5)
        * jnp.exp(-magnitude_squares / (2.0 * wall_kelvin))
    )
    inflow_magnitude_square = (
        (along_x_part - inflow_speed) ** 2
        + along_y_part * along_y_part
        + along_z_part * along_z_part
    )[:, None, None]
    inflow_distribution = (
        inflow_concentration
        * inflow_kelvin ** (-1.5)
        * jnp.exp(-inflow_magnitude_square / (2.0 * inflow_kelvin))
    )
    revised_distribution = jnp.where(
        kind_labels == 1,
        wall_distribution,
        jnp.where(kind_labels == 2, inflow_distribution, relaxed),
    )
    return (revised_distribution, kelvin_level)


def per_device(initial, site_kind):
    amount = initial.shape[0]
    along_x_part, along_y_part, along_z_part = speeds(lax.axis_index("vel") * amount, amount)
    distribution_table = initial
    kelvin_level = jnp.zeros(site_kind.shape, jnp.float32)
    for section in range(STEPS):
        padded = with_halo(distribution_table, (("space", 1),), 2)
        advected_distribution = transport(padded, along_x_part, along_y_part)
        distribution_table, kelvin_level = approach_increment(
            advected_distribution, site_kind, along_x_part, along_y_part, along_z_part
        )
    return (distribution_table, kelvin_level)


def solution(mesh):
    return jax.shard_map(
        per_device,
        mesh=mesh,
        in_specs=(P("vel", "space", None), P("space", None)),
        out_specs=(P("vel", "space", None), P("space", None)),
        check_vma=False,
    )
```

profile of v0, /device:TPU:38, one launch (start us, length us, event | category | flops | bytes accessed | tf_op | source)
XLA Modules:
  0.0 373.0 jit_solution(16900406047952305739)
XLA Ops:
  0.6 1.6 copy.19
  2.2 1.3 fusion.116
  3.5 8.0 %collective-permute-start.1 = (f32[864,2,128]{2,0,1:T(8,128)}, f32[864,2,128]{2,0,1:T(8,128)}, u32[]{:S(2)}, u32[]{:S(2)}) collective-permute-start(f32[864,2,128]{2,0,1:T(8,128)} %get-tuple-element.21), channel_id=1, source_target_pairs={{1,0},{2,1},{3,2},{4,3},{5,4},{6,5},{7,6},{8,7},{9,8},{10,9},{11,1... | collective-permute-start | bytes 2654216 | tf_op jit(solution)/shard_map/ppermute | solution.py:28
  11.6 1.9 collective-permute-start
  14.9 1.3 stack.36
  18.3 33.8 %collective-permute-done = f32[864,2,128]{2,0,1:T(8,128)} collective-permute-done((f32[864,2,128]{2,0,1:T(8,128)}, f32[864,2,128]{2,0,1:T(8,128)}, u32[]{:S(2)}, u32[]{:S(2)}) %collective-permute-start) | collective-permute-done | bytes 884768 | tf_op jit(solution)/shard_map/ppermute | solution.py:25
  56.1 2.0 fusion.16
  58.3 1.9 fusion.3
  60.2 2.4 minimum_multiply_fusion.1
  62.7 2.6 fusion.2
  67.0 70.9 %psum.28 = f32[5,4,128]{2,0,1:T(8,128)S(1)} all-reduce(f32[5,4,128]{2,0,1:T(8,128)S(1)} %fusion.74), channel_id=1, replica_groups=mesh['vel'=16,'space'=16] {'vel'}, use_global_device_ids=true, to_apply=%region_0.1 | all-reduce | flops 2560 | bytes 20480 | tf_op jit(solution)/shard_map/psum | solution.py:85
  139.1 44.3 %psum.29 = f32[3,4,128]{2,1,0:T(4,128)S(1)} all-reduce(f32[3,4,128]{2,1,0:T(4,128)S(1)} %pad_maximum_fusion.5), channel_id=1, replica_groups=mesh['vel'=16,'space'=16] {'vel'}, use_global_device_ids=true, to_apply=%region_4.5 | all-reduce | flops 1536 | bytes 12288 | tf_op jit(solution)/shard_map/psum | solution.py:114
  183.4 4.3 %fusion.42 = f32[864,4,128]{2,0,1:T(8,128)S(1)} fusion(f32[864,4,128]{2,0,1:T(8,128)S(1)} %fusion.70, f32[4,128]{1,0:T(4,128)S(1)} %bitcast.109, f32[4,128]{1,0:T(4,128)S(1)} %bitcast.115, f32[4,128]{1,0:T(4,128)S(1)} %get-tuple-element.37, f32[4,128]{1,0:T(4,128)S(1)} %get-tuple-element.38, f32[4,128]{1,0:T(4,128)S(1)} %get-tuple-element.36, ...), kind=kLoop, calls=%fused_computation.87 | loop fusion | flops 12828672 | bytes 3581824 | tf_op jit(solution)/shard_map/jit(_where)/select_n | solution.py:182
  187.8 1.9 collective-permute-start.2
  189.8 8.4 %collective-permute-start.3 = (f32[864,2,128]{2,0,1:T(8,128)S(1)}, f32[864,2,128]{2,0,1:T(8,128)S(1)}, u32[]{:S(2)}, u32[]{:S(2)}) collective-permute-start(f32[864,2,128]{2,0,1:T(8,128)S(1)} %get-tuple-element.20), channel_id=1, source_target_pairs={{1,0},{2,1},{3,2},{4,3},{5,4},{6,5},{7,6},{8,7},{9,8},{10,9},{11,1... | collective-permute-start | bytes 2654216 | tf_op jit(solution)/shard_map/ppermute | solution.py:28
  198.2 34.0 %collective-permute-done.2 = f32[864,2,128]{2,0,1:T(8,128)S(1)} collective-permute-done((f32[864,2,128]{2,0,1:T(8,128)S(1)}, f32[864,2,128]{2,0,1:T(8,128)S(1)}, u32[]{:S(2)}, u32[]{:S(2)}) %collective-permute-start.2) | collective-permute-done | bytes 884768 | tf_op jit(solution)/shard_map/ppermute | solution.py:25
  234.9 3.8 %fusion.69 = f32[864,4,128]{2,0,1:T(8,128)S(1)} fusion(f32[864,5,128]{2,0,1:T(8,128)S(1)} %fusion.12, f32[864,4,128]{2,0,1:T(8,128)S(1)} %fusion.70, f32[4,128]{1,0:T(4,128)S(1)} %bitcast.110, f32[4,128]{1,0:T(4,128)S(1)} %bitcast.116, f32[4,128]{1,0:T(4,128)S(1)} %get-tuple-element.37, f32[4,128]{1,0:T(4,128)S(1)} %get-tuple-element.38, ...), kind=kLoop, calls=%fused_computation.116 | loop fusion | flops 13713408 | bytes 7120768 | tf_op jit(solution)/shard_map/sub | solution.py:65
  238.7 1.9 fusion.8
  240.6 2.4 minimum_multiply_fusion
  243.1 2.6 fusion.7
  247.2 72.7 %psum.30 = f32[5,4,128]{2,1,0:T(4,128)S(1)} all-reduce(f32[5,4,128]{2,1,0:T(4,128)S(1)} %copy.20), channel_id=1, replica_groups=mesh['vel'=16,'space'=16] {'vel'}, use_global_device_ids=true, to_apply=%region_5.6 | all-reduce | flops 2560 | bytes 20480 | tf_op jit(solution)/shard_map/psum | solution.py:85
  321.7 44.7 %psum.31 = f32[3,4,128]{2,1,0:T(4,128)S(1)} all-reduce(f32[3,4,128]{2,1,0:T(4,128)S(1)} %pad_maximum_fusion.6), channel_id=1, replica_groups=mesh['vel'=16,'space'=16] {'vel'}, use_global_device_ids=true, to_apply=%region_9.10 | all-reduce | flops 1536 | bytes 12288 | tf_op jit(solution)/shard_map/psum | solution.py:114
  366.4 4.3 %fusion.67 = f32[864,4,128]{2,0,1:T(8,128)S(1)} fusion(f32[864,4,128]{2,0,1:T(8,128)S(1)} %fusion.68, f32[4,128]{1,0:T(4,128)S(1)} %bitcast.119, f32[4,128]{1,0:T(4,128)S(1)} %bitcast.121, f32[4,128]{1,0:T(4,128)S(1)} %get-tuple-element.34, f32[4,128]{1,0:T(4,128)S(1)} %get-tuple-element.35, f32[4,128]{1,0:T(4,128)S(1)} %get-tuple-element.33, ...), kind=kLoop, calls=%fused_computation.112 | loop fusion | flops 12828672 | bytes 3581824 | tf_op jit(solution)/shard_map/jit(_where)/select_n | solution.py:182
  370.6 2.3 copy.28
  (83 shorter events, 16.5 us)
Async XLA Ops:
  3.5 49.8 %copy-start = (f32[864,4,128]{2,1,0:T(4,128)S(1)}, f32[864,4,128]{2,1,0:T(4,128)}, u32[]{:S(2)}) copy-start(f32[864,4,128]{2,1,0:T(4,128)} %param.2) | copy-start | bytes 5308420
  3.5 49.9 %collective-permute-start.1 = (f32[864,2,128]{2,0,1:T(8,128)}, f32[864,2,128]{2,0,1:T(8,128)}, u32[]{:S(2)}, u32[]{:S(2)}) collective-permute-start(f32[864,2,128]{2,0,1:T(8,128)} %get-tuple-element.21), channel_id=1, source_target_pairs={{1,0},{2,1},{3,2},{4,3},{5,4},{6,5},{7,6},{8,7},{9,8},{10,9},{11,1... | collective-permute-start | bytes 2654216 | tf_op jit(solution)/shard_map/ppermute | solution.py:28
  11.6 40.5 %collective-permute-start = (f32[864,2,128]{2,0,1:T(8,128)}, f32[864,2,128]{2,0,1:T(8,128)}, u32[]{:S(2)}, u32[]{:S(2)}) collective-permute-start(f32[864,2,128]{2,0,1:T(8,128)} %get-tuple-element.22), channel_id=1, source_target_pairs={{0,1},{1,2},{2,3},{3,4},{4,5},{5,6},{6,7},{7,8},{8,9},{9,10},{10,1... | collective-permute-start | bytes 2654216 | tf_op jit(solution)/shard_map/ppermute | solution.py:25
  16.2 46.4 %copy-start.3 = (f32[864]{0:T(1024)}, f32[864]{0:T(1024)S(1)}, u32[]{:S(2)}) copy-start(f32[864]{0:T(1024)S(1)} %get-tuple-element.51) | copy-start | bytes 10372
  16.2 46.4 %copy-start.5 = (f32[864]{0:T(1024)}, f32[864]{0:T(1024)S(1)}, u32[]{:S(2)}) copy-start(f32[864]{0:T(1024)S(1)} %get-tuple-element.52) | copy-start | bytes 10372
  16.3 39.8 %copy-start.13 = (f32[864]{0:T(1024)}, f32[864]{0:T(1024)S(1)}, u32[]{:S(2)}) copy-start(f32[864]{0:T(1024)S(1)} %get-tuple-element.62) | copy-start | bytes 10372
  16.3 46.4 %copy-start.7 = (f32[864]{0:T(1024)}, f32[864]{0:T(1024)S(1)}, u32[]{:S(2)}) copy-start(f32[864]{0:T(1024)S(1)} %get-tuple-element.61) | copy-start | bytes 10372
  16.9 39.1 %copy-start.15 = (pred[864]{0:T(1024)(128)(4,1)}, pred[864]{0:T(1024)(128)(4,1)S(1)}, u32[]{:S(2)}) copy-start(pred[864]{0:T(1024)(128)(4,1)S(1)} %get-tuple-element.60) | copy-start | bytes 2596
  17.0 45.7 %copy-start.17 = (pred[864]{0:T(1024)(128)(4,1)}, pred[864]{0:T(1024)(128)(4,1)S(1)}, u32[]{:S(2)}) copy-start(pred[864]{0:T(1024)(128)(4,1)S(1)} %get-tuple-element.59) | copy-start | bytes 2596
  54.9 1.2 copy-start.9
  54.9 1.2 copy-start.11
  66.0 117.4 %copy-start.2 = (f32[864]{0:T(1024)S(1)}, f32[864]{0:T(1024)}, u32[]{:S(2)}) copy-start(f32[864]{0:T(1024)} %get-tuple-element.50) | copy-start | bytes 10372
  66.0 117.4 %copy-start.19 = (pred[4,128]{1,0:T(4,128)(4,1)S(1)}, pred[4,128]{1,0:T(4,128)(4,1)}, u32[]{:S(2)}) copy-start(pred[4,128]{1,0:T(4,128)(4,1)} %get-tuple-element.45) | copy-start | bytes 1540
  66.0 117.4 %copy-start.20 = (pred[4,128]{1,0:T(4,128)(4,1)S(1)}, pred[4,128]{1,0:T(4,128)(4,1)}, u32[]{:S(2)}) copy-start(pred[4,128]{1,0:T(4,128)(4,1)} %get-tuple-element.46) | copy-start | bytes 1540
  187.8 44.4 %collective-permute-start.2 = (f32[864,2,128]{2,0,1:T(8,128)S(1)}, f32[864,2,128]{2,0,1:T(8,128)S(1)}, u32[]{:S(2)}, u32[]{:S(2)}) collective-permute-start(f32[864,2,128]{2,0,1:T(8,128)S(1)} %get-tuple-element.19), channel_id=1, source_target_pairs={{0,1},{1,2},{2,3},{3,4},{4,5},{5,6},{6,7},{7,8},{8,9},{9,10},{10,1... | collective-permute-start | bytes 2654216 | tf_op jit(solution)/shard_map/ppermute | solution.py:25
  189.8 42.4 %collective-permute-start.3 = (f32[864,2,128]{2,0,1:T(8,128)S(1)}, f32[864,2,128]{2,0,1:T(8,128)S(1)}, u32[]{:S(2)}, u32[]{:S(2)}) collective-permute-start(f32[864,2,128]{2,0,1:T(8,128)S(1)} %get-tuple-element.20), channel_id=1, source_target_pairs={{1,0},{2,1},{3,2},{4,3},{5,4},{6,5},{7,6},{8,7},{9,8},{10,9},{11,1... | collective-permute-start | bytes 2654216 | tf_op jit(solution)/shard_map/ppermute | solution.py:28
  232.7 1.2 copy-start.10
  232.7 1.2 copy-start.12
  232.7 1.2 copy-start.14
  232.7 1.2 copy-start.16
  240.6 2.5 copy-start.4
  240.6 2.5 copy-start.6
  240.6 2.5 copy-start.8
  240.6 2.5 copy-start.18
  (1 other events, 0.7 us)
where the time goes:
time: 373 us
  blocking collectives  233 us (62%)
  waiting for transfers between devices  67.8 us (18%)
  other arithmetic  39.1 us (10%)
  starting transfers between devices  20.3 us (5%)
  local copies, waits for them, and re-layouts  10.1 us (3%)
    psum x2, blocking collectives, macroscopic_moments(): integral_totals = lax.psum(local, 'vel')  144 us
    psum x2, blocking collectives, macroscopic_moments(): conductive_transfer = lax.psum(local_heat, 'vel')  89 us
    ppermute x2, waiting for transfers between devices, with_halo(): lax.ppermute(lax.slice_in_dim(block, block.shape[dim] - width, None, axis...  67.8 us
    ppermute x2, starting transfers between devices, with_halo(): lax.ppermute(lax.slice_in_dim(block, 0, width, axis=dim), axis, backward)  16.5 us
    select_n x2, other arithmetic, approach_increment(): jnp.where(kind_labels == 1, wall_distribution, jnp.where(kind_labels == 2...  8.54 us
    mul x4, other arithmetic, sweep(): flux = number * jnp.where(number > 0, left_face, right_face)  8.15 us
  transfers between devices with their start and end apart: 4, of which 2 were waited for; matrix products, arithmetic and copies ran while one was open for 2% of the time, Pallas kernels for 0%

commit v1 on v0

--- a/solution.py
+++ b/solution.py
@@ -111,7 +111,7 @@
             jnp.sum(rel_z * scaled, axis=0),
         ]
     )
-    conductive_transfer = lax.psum(local_heat, "vel")
+    conductive_transfer = jnp.sum(lax.all_gather(local_heat, "vel"), axis=0)
     return (
         particle_concentration,
         average_drift_x,

time: 373 us -> 371 us (level)
    psum x2 -> x0, blocking collectives: 89 us -> none  [macroscopic_moments(): conductive_transfer = lax.psum(local_heat, 'vel')]
    all_gather x0 -> x2, blocking collectives: none -> 86.8 us  [macroscopic_moments(): conductive_transfer = jnp.sum(lax.all_gather(local_heat, 'vel'), axis=0)]
where the time goes in v1:
time: 371 us
  blocking collectives  230 us (62%)
  waiting for transfers between devices  67.8 us (18%)
  other arithmetic  39.2 us (11%)
  starting transfers between devices  20.3 us (5%)
  local copies, waits for them, and re-layouts  10.1 us (3%)
    psum x2, blocking collectives, macroscopic_moments(): integral_totals = lax.psum(local, 'vel')  143 us
    all_gather x2, blocking collectives, macroscopic_moments(): conductive_transfer = jnp.sum(lax.all_gather(local_heat, 'vel'), axis=0)  86.8 us
    ppermute x2, waiting for transfers between devices, with_halo(): lax.ppermute(lax.slice_in_dim(block, block.shape[dim] - width, None, axis...  67.8 us
    ppermute x2, starting transfers between devices, with_halo(): lax.ppermute(lax.slice_in_dim(block, 0, width, axis=dim), axis, backward)  16.5 us
    select_n x2, other arithmetic, approach_increment(): jnp.where(kind_labels == 1, wall_distribution, jnp.where(kind_labels == 2...  8.54 us
    mul x4, other arithmetic, sweep(): flux = number * jnp.where(number > 0, left_face, right_face)  8.15 us
  transfers between devices with their start and end apart: 4, of which 2 were waited for; matrix products, arithmetic and copies ran while one was open for 2% of the time, Pallas kernels for 0%

profile of v1, /device:TPU:38, one launch (start us, length us, event | category | flops | bytes accessed | tf_op | source)
XLA Modules:
  0.0 370.7 jit_solution(13983804157824792558)
XLA Ops:
  0.6 1.6 copy.19
  2.2 1.3 fusion.116
  3.5 8.0 %collective-permute-start.1 = (f32[864,2,128]{2,0,1:T(8,128)}, f32[864,2,128]{2,0,1:T(8,128)}, u32[]{:S(2)}, u32[]{:S(2)}) collective-permute-start(f32[864,2,128]{2,0,1:T(8,128)} %get-tuple-element.21), channel_id=1, source_target_pairs={{1,0},{2,1},{3,2},{4,3},{5,4},{6,5},{7,6},{8,7},{9,8},{10,9},{11,1... | collective-permute-start | bytes 2654216 | tf_op jit(solution)/shard_map/ppermute | solution.py:28
  11.6 1.9 collective-permute-start
  14.9 1.3 stack.36
  18.3 33.8 %collective-permute-done = f32[864,2,128]{2,0,1:T(8,128)} collective-permute-done((f32[864,2,128]{2,0,1:T(8,128)}, f32[864,2,128]{2,0,1:T(8,128)}, u32[]{:S(2)}, u32[]{:S(2)}) %collective-permute-start) | collective-permute-done | bytes 884768 | tf_op jit(solution)/shard_map/ppermute | solution.py:25
  56.1 2.0 fusion.16
  58.3 1.9 fusion.3
  60.2 2.4 minimum_multiply_fusion.1
  62.7 2.6 fusion.2
  67.0 70.9 %psum.14 = f32[5,4,128]{2,0,1:T(8,128)S(1)} all-reduce(f32[5,4,128]{2,0,1:T(8,128)S(1)} %fusion.74), channel_id=1, replica_groups=mesh['vel'=16,'space'=16] {'vel'}, use_global_device_ids=true, to_apply=%region_0.1 | all-reduce | flops 2560 | bytes 20480 | tf_op jit(solution)/shard_map/psum | solution.py:85
  139.1 43.2 %all-gather = f32[48,4,128]{2,1,0:T(4,128)S(1)} all-gather(f32[3,4,128]{2,1,0:T(4,128)S(1)} %pad_maximum_fusion.5), channel_id=2, replica_groups=mesh['vel'=16,'space'=16] {'vel'}, dimensions={0}, use_global_device_ids=true | all-gather | bytes 104448 | tf_op jit(solution)/shard_map/all_gather | solution.py:114
  182.4 4.3 %fusion.42 = f32[864,4,128]{2,0,1:T(8,128)S(1)} fusion(f32[864,4,128]{2,0,1:T(8,128)S(1)} %fusion.70, f32[4,128]{1,0:T(4,128)S(1)} %bitcast.113, f32[4,128]{1,0:T(4,128)S(1)} %bitcast.119, f32[4,128]{1,0:T(4,128)S(1)} %get-tuple-element.37, f32[4,128]{1,0:T(4,128)S(1)} %get-tuple-element.38, f32[4,128]{1,0:T(4,128)S(1)} %get-tuple-element.36, ...), kind=kLoop, calls=%fused_computation.87 | loop fusion | flops 12828672 | bytes 3581824 | tf_op jit(solution)/shard_map/jit(_where)/select_n | solution.py:182
  186.8 1.9 collective-permute-start.2
  188.7 8.4 %collective-permute-start.3 = (f32[864,2,128]{2,0,1:T(8,128)S(1)}, f32[864,2,128]{2,0,1:T(8,128)S(1)}, u32[]{:S(2)}, u32[]{:S(2)}) collective-permute-start(f32[864,2,128]{2,0,1:T(8,128)S(1)} %get-tuple-element.20), channel_id=1, source_target_pairs={{1,0},{2,1},{3,2},{4,3},{5,4},{6,5},{7,6},{8,7},{9,8},{10,9},{11,1... | collective-permute-start | bytes 2654216 | tf_op jit(solution)/shard_map/ppermute | solution.py:28
  197.2 34.0 %collective-permute-done.2 = f32[864,2,128]{2,0,1:T(8,128)S(1)} collective-permute-done((f32[864,2,128]{2,0,1:T(8,128)S(1)}, f32[864,2,128]{2,0,1:T(8,128)S(1)}, u32[]{:S(2)}, u32[]{:S(2)}) %collective-permute-start.2) | collective-permute-done | bytes 884768 | tf_op jit(solution)/shard_map/ppermute | solution.py:25
  233.8 3.8 %fusion.69 = f32[864,4,128]{2,0,1:T(8,128)S(1)} fusion(f32[864,5,128]{2,0,1:T(8,128)S(1)} %fusion.12, f32[864,4,128]{2,0,1:T(8,128)S(1)} %fusion.70, f32[4,128]{1,0:T(4,128)S(1)} %bitcast.114, f32[4,128]{1,0:T(4,128)S(1)} %bitcast.120, f32[4,128]{1,0:T(4,128)S(1)} %get-tuple-element.37, f32[4,128]{1,0:T(4,128)S(1)} %get-tuple-element.38, ...), kind=kLoop, calls=%fused_computation.116 | loop fusion | flops 13713408 | bytes 7120768 | tf_op jit(solution)/shard_map/sub | solution.py:65
  237.7 1.9 fusion.8
  239.6 2.4 minimum_multiply_fusion
  242.1 2.6 fusion.7
  246.1 72.5 %psum.15 = f32[5,4,128]{2,1,0:T(4,128)S(1)} all-reduce(f32[5,4,128]{2,1,0:T(4,128)S(1)} %copy.20), channel_id=1, replica_groups=mesh['vel'=16,'space'=16] {'vel'}, use_global_device_ids=true, to_apply=%region_5.6 | all-reduce | flops 2560 | bytes 20480 | tf_op jit(solution)/shard_map/psum | solution.py:85
  320.5 43.6 %all-gather.1 = f32[48,4,128]{2,1,0:T(4,128)S(1)} all-gather(f32[3,4,128]{2,1,0:T(4,128)S(1)} %pad_maximum_fusion.6), channel_id=3, replica_groups=mesh['vel'=16,'space'=16] {'vel'}, dimensions={0}, use_global_device_ids=true | all-gather | bytes 104448 | tf_op jit(solution)/shard_map/all_gather | solution.py:114
  364.1 4.3 %fusion.67 = f32[864,4,128]{2,0,1:T(8,128)S(1)} fusion(f32[864,4,128]{2,0,1:T(8,128)S(1)} %fusion.68, f32[4,128]{1,0:T(4,128)S(1)} %bitcast.123, f32[4,128]{1,0:T(4,128)S(1)} %bitcast.125, f32[4,128]{1,0:T(4,128)S(1)} %get-tuple-element.34, f32[4,128]{1,0:T(4,128)S(1)} %get-tuple-element.35, f32[4,128]{1,0:T(4,128)S(1)} %get-tuple-element.33, ...), kind=kLoop, calls=%fused_computation.112 | loop fusion | flops 12828672 | bytes 3581824 | tf_op jit(solution)/shard_map/jit(_where)/select_n | solution.py:182
  368.3 2.3 copy.28
  (85 shorter events, 16.5 us)
Async XLA Ops:
  3.5 49.8 %copy-start = (f32[864,4,128]{2,1,0:T(4,128)S(1)}, f32[864,4,128]{2,1,0:T(4,128)}, u32[]{:S(2)}) copy-start(f32[864,4,128]{2,1,0:T(4,128)} %param.2) | copy-start | bytes 5308420
  3.5 49.9 %collective-permute-start.1 = (f32[864,2,128]{2,0,1:T(8,128)}, f32[864,2,128]{2,0,1:T(8,128)}, u32[]{:S(2)}, u32[]{:S(2)}) collective-permute-start(f32[864,2,128]{2,0,1:T(8,128)} %get-tuple-element.21), channel_id=1, source_target_pairs={{1,0},{2,1},{3,2},{4,3},{5,4},{6,5},{7,6},{8,7},{9,8},{10,9},{11,1... | collective-permute-start | bytes 2654216 | tf_op jit(solution)/shard_map/ppermute | solution.py:28
  11.6 40.5 %collective-permute-start = (f32[864,2,128]{2,0,1:T(8,128)}, f32[864,2,128]{2,0,1:T(8,128)}, u32[]{:S(2)}, u32[]{:S(2)}) collective-permute-start(f32[864,2,128]{2,0,1:T(8,128)} %get-tuple-element.22), channel_id=1, source_target_pairs={{0,1},{1,2},{2,3},{3,4},{4,5},{5,6},{6,7},{7,8},{8,9},{9,10},{10,1... | collective-permute-start | bytes 2654216 | tf_op jit(solution)/shard_map/ppermute | solution.py:25
  16.2 46.4 %copy-start.3 = (f32[864]{0:T(1024)}, f32[864]{0:T(1024)S(1)}, u32[]{:S(2)}) copy-start(f32[864]{0:T(1024)S(1)} %get-tuple-element.51) | copy-start | bytes 10372
  16.2 46.4 %copy-start.5 = (f32[864]{0:T(1024)}, f32[864]{0:T(1024)S(1)}, u32[]{:S(2)}) copy-start(f32[864]{0:T(1024)S(1)} %get-tuple-element.52) | copy-start | bytes 10372
  16.3 39.8 %copy-start.13 = (f32[864]{0:T(1024)}, f32[864]{0:T(1024)S(1)}, u32[]{:S(2)}) copy-start(f32[864]{0:T(1024)S(1)} %get-tuple-element.62) | copy-start | bytes 10372
  16.3 46.4 %copy-start.7 = (f32[864]{0:T(1024)}, f32[864]{0:T(1024)S(1)}, u32[]{:S(2)}) copy-start(f32[864]{0:T(1024)S(1)} %get-tuple-element.61) | copy-start | bytes 10372
  16.9 39.1 %copy-start.15 = (pred[864]{0:T(1024)(128)(4,1)}, pred[864]{0:T(1024)(128)(4,1)S(1)}, u32[]{:S(2)}) copy-start(pred[864]{0:T(1024)(128)(4,1)S(1)} %get-tuple-element.60) | copy-start | bytes 2596
  17.0 45.7 %copy-start.17 = (pred[864]{0:T(1024)(128)(4,1)}, pred[864]{0:T(1024)(128)(4,1)S(1)}, u32[]{:S(2)}) copy-start(pred[864]{0:T(1024)(128)(4,1)S(1)} %get-tuple-element.59) | copy-start | bytes 2596
  54.9 1.2 copy-start.9
  54.9 1.2 copy-start.11
  66.0 116.3 %copy-start.2 = (f32[864]{0:T(1024)S(1)}, f32[864]{0:T(1024)}, u32[]{:S(2)}) copy-start(f32[864]{0:T(1024)} %get-tuple-element.50) | copy-start | bytes 10372
  66.0 116.3 %copy-start.19 = (pred[4,128]{1,0:T(4,128)(4,1)S(1)}, pred[4,128]{1,0:T(4,128)(4,1)}, u32[]{:S(2)}) copy-start(pred[4,128]{1,0:T(4,128)(4,1)} %get-tuple-element.45) | copy-start | bytes 1540
  66.0 116.3 %copy-start.20 = (pred[4,128]{1,0:T(4,128)(4,1)S(1)}, pred[4,128]{1,0:T(4,128)(4,1)}, u32[]{:S(2)}) copy-start(pred[4,128]{1,0:T(4,128)(4,1)} %get-tuple-element.46) | copy-start | bytes 1540
  186.8 44.4 %collective-permute-start.2 = (f32[864,2,128]{2,0,1:T(8,128)S(1)}, f32[864,2,128]{2,0,1:T(8,128)S(1)}, u32[]{:S(2)}, u32[]{:S(2)}) collective-permute-start(f32[864,2,128]{2,0,1:T(8,128)S(1)} %get-tuple-element.19), channel_id=1, source_target_pairs={{0,1},{1,2},{2,3},{3,4},{4,5},{5,6},{6,7},{7,8},{8,9},{9,10},{10,1... | collective-permute-start | bytes 2654216 | tf_op jit(solution)/shard_map/ppermute | solution.py:25
  188.7 42.5 %collective-permute-start.3 = (f32[864,2,128]{2,0,1:T(8,128)S(1)}, f32[864,2,128]{2,0,1:T(8,128)S(1)}, u32[]{:S(2)}, u32[]{:S(2)}) collective-permute-start(f32[864,2,128]{2,0,1:T(8,128)S(1)} %get-tuple-element.20), channel_id=1, source_target_pairs={{1,0},{2,1},{3,2},{4,3},{5,4},{6,5},{7,6},{8,7},{9,8},{10,9},{11,1... | collective-permute-start | bytes 2654216 | tf_op jit(solution)/shard_map/ppermute | solution.py:28
  231.6 1.2 copy-start.10
  231.6 1.2 copy-start.12
  231.6 1.2 copy-start.14
  231.7 1.2 copy-start.16
  239.6 2.5 copy-start.4
  239.6 2.5 copy-start.6
  239.6 2.5 copy-start.8
  239.6 2.5 copy-start.18
  (1 other events, 0.7 us)
